TPU v7x, 32 devices: a whole 2x2x4 slice. The times are simulated.
32 devices in a mesh: row: 8 (over y, x, core), col: 4 (over z).
Axes of the slice: x: 2, y: 2, z: 4, core: 2. Of those that a mesh axis runs over, the one named last changes fastest.
Arguments:
- queries: bfloat16 [512, 2, 2048], P('row', None, 'col'), may hold values from -15 to 15
- new_keys: bfloat16 [512, 2, 2048], P('row', None, 'col'), may hold values from -6 to 6
- new_values: bfloat16 [512, 2, 2048], P('row', None, 'col'), may hold values from -6 to 6
- cache_keys: bfloat16 [1024, 2, 2048], P('row', None, 'col'), may hold values from -6 to 6
- cache_values: bfloat16 [1024, 2, 2048], P('row', None, 'col'), may hold values from -6 to 6
- cached_len: int32 [2], replicated, may hold values from 256 to 1024, as said below
- residual: bfloat16 [512, 2, 2048], P('row'), may hold values from -4 to 4
- out_weight: bfloat16 [2048, 2048], P('col'), may hold values from -0.125 to 0.125
- norm_gain: float32 [2048], replicated, may hold values from 0.5 to 1.5
- expert_ids: int32 [512, 2, 6], P('row'), may hold values from 0 to 63, all different within a row; in each aligned block of 128 rows (0 to 127, 128 to 255, ..., all dimensions but the last counted through in order) at most 24 rows name the same one
- gate_values: float32 [512, 2, 6], P('row'), may hold values from 0.1 to 0.6
- w_gate: bfloat16 [256, 2048, 352], P(('row', 'col')), may hold values from -0.125 to 0.125
- w_up: bfloat16 [256, 2048, 352], P(('row', 'col')), may hold values from -0.125 to 0.125
- w_down: bfloat16 [256, 352, 2048], P(('row', 'col')), may hold values from -0.15625 to 0.15625
- shared_gate: bfloat16 [2048, 2816], P(None, 'col'), may hold values from -0.125 to 0.125
- shared_up: bfloat16 [2048, 2816], P(None, 'col'), may hold values from -0.125 to 0.125
- shared_down: bfloat16 [2816, 2048], P('col'), may hold values from -0.109375 to 0.109375
Outputs:
- mixed: bfloat16 [512, 2, 2048], P('row', None, 'col')
- ffn_out: bfloat16 [512, 2, 2048], P('row', None, 'col')
Inputs may be any that keep to these rules, and one draw needn't show every extreme that they name: `cached_len`: some request has exactly 1024 cached positions. `expert_ids`: each token names 6 different experts. Among the 128 tokens of one index of row (positions taken in order, requests inside), no expert is named more than 24 times, and in some such blocks one expert is named exactly 24 times.
All inputs are finite; a program needn't handle non-finite values.
Results may differ from a plain program's by a relative error of at most 0.023.
Values may be sent and summed in bfloat16 or wider, within the bound.
No kernel may reach another device: no remote copies, remote signals or barrier semaphores. Data moves between devices by JAX's collectives and lax.ppermute only.
A program may use at most 192 MiB of HBM per device.

v0:
```python
import math
import jax
import jax.numpy as jnp
from jax import lax
from jax.sharding import PartitionSpec as P

HD = 128
E = 64
TOPK = 6
GROUPS = 4
CAP = 24


def body(
    queries,
    new_keys,
    new_values,
    cache_keys,
    cache_values,
    cached_len,
    residual,
    out_weight,
    norm_gain,
    expert_ids,
    gate_values,
    w_gate,
    w_up,
    w_down,
    shared_gate,
    shared_up,
    shared_down,
):
    rows_here = queries.shape[0]
    requests = queries.shape[1]
    heads_here = queries.shape[2] // HD
    cache_rows = cache_keys.shape[0]
    block_rows = cache_rows + rows_here
    model_width = residual.shape[2]
    row_index = lax.axis_index("row")
    row_count = lax.axis_size("row")
    score_scale = 1.0 / math.sqrt(HD)
    keys_here = jnp.concatenate([cache_keys, new_keys], axis=0)
    values_here = jnp.concatenate([cache_values, new_values], axis=0)
    query_heads = queries.reshape(rows_here, requests, heads_here, HD)
    local_pos = row_index * rows_here + jnp.arange(rows_here, dtype=jnp.int32)
    key_piece = lax.all_gather(keys_here, "row", axis=0, tiled=True)
    key_count = key_piece.shape[0]
    global_row = jnp.arange(key_count, dtype=jnp.int32)
    shard_index = global_row // block_rows
    offset_rows = global_row % block_rows
    in_cache = offset_rows < cache_rows
    cache_pos = shard_index * cache_rows + offset_rows
    new_pos = shard_index * rows_here + offset_rows - cache_rows
    cache_ok = in_cache[None, :] & (cache_pos[None, :] < cached_len[:, None])
    new_ok = jnp.logical_not(in_cache)[None, :] & (new_pos[None, :] <= local_pos[:, None])
    allowed = cache_ok[:, None, None, :] | new_ok[None, None, :, :]
    key_heads = key_piece.reshape(key_count, requests, heads_here, HD)
    value_heads = lax.all_gather(values_here, "row", axis=0, tiled=True).reshape(
        key_count, requests, heads_here, HD
    )
    scores = (
        jnp.einsum("irhd,jrhd->rhij", query_heads, key_heads, preferred_element_type=jnp.float32)
        * score_scale
    )
    masked = jnp.where(allowed, scores, -1e30)
    old_max = jnp.full((requests, heads_here, rows_here), -1e30, jnp.float32)
    new_max = jnp.maximum(old_max, jnp.max(masked, axis=-1))
    weights_now = jnp.where(allowed, jnp.exp(masked - new_max[..., None]), 0.0)
    new_sum = jnp.sum(weights_now, axis=-1)
    product = jnp.einsum(
        "rhij,jrhd->rhid",
        weights_now.astype(jnp.bfloat16),
        value_heads,
        preferred_element_type=jnp.float32,
    )
    attended = (product / new_sum[..., None]).astype(jnp.bfloat16)
    head_weights = out_weight.reshape(heads_here, HD, model_width)
    attn_part = jnp.einsum(
        "rhid,hde->ire", attended, head_weights, preferred_element_type=jnp.float32
    )
    attn_full = lax.psum(attn_part.astype(jnp.bfloat16), "col").astype(jnp.float32)
    mixed_full = (residual.astype(jnp.float32) + attn_full).astype(jnp.bfloat16)
    mixed_f32 = mixed_full.astype(jnp.float32)
    normed = (
        mixed_f32
        * lax.rsqrt(jnp.mean(mixed_f32 * mixed_f32, axis=-1, keepdims=True) + 1e-06)
        * norm_gain
    ).astype(jnp.bfloat16)
    token_count = rows_here * requests
    tokens = normed.reshape(token_count, model_width)
    col_index = lax.axis_index("col")
    col_count = lax.axis_size("col")
    entries_here = w_gate.shape[0]
    experts_dev = max(1, entries_here // GROUPS)
    groups_dev = entries_here // experts_dev
    experts_per_row = col_count * entries_here // GROUPS
    slots = row_count * experts_dev * CAP
    chosen = expert_ids.reshape(token_count * TOPK)
    onehot = (chosen[:, None] == jnp.arange(E, dtype=jnp.int32)[None, :]).astype(jnp.int32)
    slot_index = jnp.sum(jnp.cumsum(onehot, axis=0) * onehot, axis=1) - 1
    dest_row = chosen // experts_per_row
    local_expert = chosen - (dest_row * col_count + col_index) * entries_here // GROUPS
    valid = (local_expert >= 0) & (local_expert < experts_dev)
    place = (dest_row * experts_dev + local_expert) * CAP + slot_index
    place = jnp.where(valid, place, -1).reshape(token_count, TOPK)
    hit = place[:, :, None] == jnp.arange(slots, dtype=jnp.int32)[None, None, :]
    dispatch = jnp.sum(hit.astype(jnp.float32), axis=1).astype(jnp.bfloat16)
    combine = jnp.sum(jnp.where(hit, gate_values.reshape(token_count, TOPK, 1), 0.0), axis=1)
    outgoing = lax.dot_general(
        dispatch, tokens, (((0,), (0,)), ((), ())), preferred_element_type=jnp.float32
    ).astype(jnp.bfloat16)
    outgoing = outgoing.reshape(row_count, experts_dev, CAP, model_width)
    arrived = lax.all_to_all(outgoing, "row", 0, 0, tiled=True)
    hidden = w_gate.shape[2]
    wg = w_gate.reshape(experts_dev, groups_dev, model_width, hidden)
    wu = w_up.reshape(experts_dev, groups_dev, model_width, hidden)
    wd = w_down.reshape(experts_dev, groups_dev, hidden, model_width)
    gate_proj = jnp.einsum("nlsd,lgdf->lgnsf", arrived, wg, preferred_element_type=jnp.float32)
    up_proj = jnp.einsum("nlsd,lgdf->lgnsf", arrived, wu, preferred_element_type=jnp.float32)
    hidden_act = (jax.nn.silu(gate_proj) * up_proj).astype(jnp.bfloat16)
    expert_out = jnp.einsum(
        "lgnsf,lgfd->nlsd", hidden_act, wd, preferred_element_type=jnp.float32
    ).astype(jnp.bfloat16)
    returned = lax.all_to_all(expert_out, "row", 0, 0, tiled=True).reshape(slots, model_width)
    combine_hi = combine.astype(jnp.bfloat16)
    combine_lo = (combine - combine_hi.astype(jnp.float32)).astype(jnp.bfloat16)
    routed = jnp.dot(combine_hi, returned, preferred_element_type=jnp.float32) + jnp.dot(
        combine_lo, returned, preferred_element_type=jnp.float32
    )
    shared_g = jnp.dot(tokens, shared_gate, preferred_element_type=jnp.float32)
    shared_u = jnp.dot(tokens, shared_up, preferred_element_type=jnp.float32)
    shared_act = (jax.nn.silu(shared_g) * shared_u).astype(jnp.bfloat16)
    shared_part = jnp.dot(shared_act, shared_down, preferred_element_type=jnp.float32)
    ffn_total = lax.psum_scatter(
        (routed + shared_part).astype(jnp.bfloat16), "col", scatter_dimension=1, tiled=True
    )
    col_width = model_width // col_count
    ffn_here = ffn_total.reshape(rows_here, requests, col_width)
    mixed_here = lax.dynamic_slice_in_dim(mixed_full, col_index * col_width, col_width, 2)
    return (mixed_here, ffn_here)


def solution(mesh):
    in_specs = (
        P("row", None, "col"),
        P("row", None, "col"),
        P("row", None, "col"),
        P("row", None, "col"),
        P("row", None, "col"),
        P(),
        P("row", None, None),
        P("col", None),
        P(),
        P("row", None, None),
        P("row", None, None),
        P(("row", "col"), None, None),
        P(("row", "col"), None, None),
        P(("row", "col"), None, None),
        P(None, "col"),
        P(None, "col"),
        P("col", None),
    )
    out_specs = (P("row", None, "col"), P("row", None, "col"))
    return jax.shard_map(body, mesh=mesh, in_specs=in_specs, out_specs=out_specs, check_vma=False)
```

profile of v0, /device:TPU:0, one launch (start us, length us, event | category | flops | bytes accessed | tf_op | source)
XLA Modules:
  0.0 250.1 jit_solution(14127599166133961431)
XLA Ops:
  7.2 2.4 pad_maximum_fusion
  9.8 2.3 pad_maximum_fusion.1
  14.2 1.8 reduce-window.6
  16.9 28.1 %all-gather.3.cloned.1.call-done = bf16[1536,2,512]{2,1,0:T(2,128)(2,1)} async-done(((bf16[192,2,512]{2,1,0:T(2,128)(2,1)}), bf16[1536,2,512]{2,1,0:T(2,128)(2,1)}) %all-gather.3.cloned.1.call-update) | async-done | bytes 3145744 | tf_op jit(solution)/shard_map/all_gather | solution.py:46
  45.0 8.7 %copy.68 = bf16[1536,2,512]{0,2,1:T(8,128)(2,1)} copy(bf16[1536,2,512]{2,1,0:T(2,128)(2,1)} %all-gather.3.cloned.1.call-done) | data formatting | bytes 6291456 | tf_op jit(solution)/shard_map/all_gather | solution.py:46
  53.7 3.0 %fusion.62 = (f32[2,4,64]{2,1,0:T(4,128)S(1)}, f32[2,4,64,1536]{3,2,1,0:T(8,128)S(1)}) fusion(bf16[1536,2,4,128]{0,3,2,1:T(8,128)(2,1)} %bitcast.114, bf16[64,2,4,128]{3,2,1,0:T(4,128)(2,1)S(1)} %reshape.257, pred[2,64,1536]{2,1,0:T(8,128)(4,1)S(1)} %broadcast_or_fusion), kind=kOutput, calls=%fused_computation.106 | convolution fusion | flops 203685376 | bytes 6621184 | tf_op jit(solution)/shard_map/irhd,jrhd->rhij/dot_general | solution.py:62
  56.7 1.7 copy-done.1
  59.2 20.0 %all-gather.5.cloned.1.call-done = bf16[1536,2,512]{2,1,0:T(2,128)(2,1)} async-done(((bf16[192,2,512]{2,1,0:T(2,128)(2,1)}), bf16[1536,2,512]{2,1,0:T(2,128)(2,1)}) %all-gather.5.cloned.1.call-update) | async-done | bytes 3145744 | tf_op jit(solution)/shard_map/all_gather | solution.py:58
  79.2 8.7 %copy.71 = bf16[1536,2,512]{0,2,1:T(8,128)(2,1)} copy(bf16[1536,2,512]{2,1,0:T(2,128)(2,1)} %all-gather.5.cloned.1.call-done) | data formatting | bytes 6291456 | tf_op jit(solution)/shard_map/all_gather | solution.py:58
  87.9 5.9 %fusion.11 = bf16[64,2,2048]{2,0,1:T(8,128)(2,1)} fusion(bf16[4,128,2048,1]{2,1,0,3:T(8,128)(2,1)} %bitcast.123, bf16[1536,2,4,128]{0,3,2,1:T(8,128)(2,1)} %bitcast.116, f32[2,4,64,1536]{3,2,1,0:T(8,128)} %copy-done.1, f32[2,4,64]{2,1,0:T(4,128)S(1)} %broadcast_maximum_fusion, pred[2,64,1536]{2,1,0:T(8,128)(4,1)S(1)} %broadcast_or_fusion, ...), kind=kOutput, calls=%fused_computation.21 | convolution fusion | flops 472514560 | bytes 9113600 | tf_op jit(solution)/shard_map/rhid,hde->ire/dot_general | solution.py:78
  95.3 37.0 %all-reduce.2.cloned.1.call-done = bf16[64,2,2048]{2,0,1:T(8,128)(2,1)} async-done(((bf16[64,2,2048]{2,0,1:T(8,128)(2,1)}), bf16[64,2,2048]{2,0,1:T(8,128)(2,1)}) %all-reduce.2.cloned.1.call-update) | async-done | bytes 524304 | tf_op jit(solution)/shard_map/psum | solution.py:81
  132.3 1.5 fusion.29
  138.0 24.4 %all_to_all.10 = bf16[8,2,24,2048]{3,2,1,0:T(8,128)(2,1)S(1)} all-to-all(bf16[8,2,24,2048]{3,2,1,0:T(8,128)(2,1)S(1)} %bitcast.115), channel_id=1, replica_groups=mesh['row'=8,'col'=4] {'row'}, dimensions={0} | all-to-all | bytes 3145728 | tf_op jit(solution)/shard_map/all_to_all | solution.py:113
  162.4 8.5 %fusion.17 = f32[2,8,24,4,352]{4,2,3,1,0:T(8,128)} fusion(bf16[2,4,2048,352,1]{2,3,1,4,0:T(8,128)(2,1)} %bitcast.120, bf16[8,2,24,2048]{3,2,1,0:T(8,128)(2,1)S(1)} %all_to_all.10), kind=kOutput, calls=%fused_computation.26 | convolution fusion | flops 2214592512 | bytes 15269888 | tf_op jit(solution)/shard_map/nlsd,lgdf->lgnsf/dot_general | solution.py:119
  171.0 12.9 %fusion.2 = bf16[8,2,24,2048]{3,2,0,1:T(8,128)(2,1)} fusion(bf16[2,4,352,2048,1]{3,2,1,4,0:T(8,128)(2,1)} %bitcast.121, f32[2,8,24,4,352]{4,2,3,1,0:T(8,128)} %fusion.17, bf16[2,4,2048,352,1]{2,3,1,4,0:T(8,128)(2,1)} %bitcast.122, bf16[8,2,24,2048]{3,2,1,0:T(8,128)(2,1)} %copy-done.4), kind=kOutput, calls=%fused_computation.6 | convolution fusion | flops 4433215488 | bytes 28377088 | tf_op jit(solution)/shard_map/lgnsf,lgfd->nlsd/dot_general | solution.py:121
  183.9 2.7 %copy.83 = bf16[8,2,24,2048]{3,2,1,0:T(8,128)(2,1)} copy(bf16[8,2,24,2048]{3,2,0,1:T(8,128)(2,1)} %fusion.2) | data formatting | bytes 3145728 | tf_op jit(solution)/shard_map/convert_element_type | solution.py:123
  186.6 4.3 %all-to-all-start.1 = ((bf16[8,2,24,2048]{3,2,1,0:T(8,128)(2,1)}), bf16[8,2,24,2048]{3,2,1,0:T(8,128)(2,1)}, u32[]{:S(2)}, u32[]{:S(2)}) async-start(bf16[8,2,24,2048]{3,2,1,0:T(8,128)(2,1)} %copy.83), calls=%async_computation.1 | async-start | bytes 3145728 | tf_op jit(solution)/shard_map/all_to_all | solution.py:124
  191.0 3.5 %fusion.63 = f32[128,704]{0,1:T(8,128)} fusion(bf16[128,2048]{1,0:T(8,128)(2,1)S(1)} %reshape.262, bf16[2048,704]{0,1:T(8,128)(2,1)} %param.31), kind=kOutput, calls=%fused_computation.107 | convolution fusion | flops 369098752 | bytes 3768320 | tf_op jit(solution)/shard_map/dot_general | solution.py:130
  194.4 17.5 %all-to-all-done.1 = bf16[8,2,24,2048]{3,2,1,0:T(8,128)(2,1)} async-done(((bf16[8,2,24,2048]{3,2,1,0:T(8,128)(2,1)}), bf16[8,2,24,2048]{3,2,1,0:T(8,128)(2,1)}, u32[]{:S(2)}, u32[]{:S(2)}) %all-to-all-start.1) | async-done | bytes 1572896 | tf_op jit(solution)/shard_map/all_to_all | solution.py:124
  212.0 2.0 fusion.50
  214.0 2.8 %convolution_add_fusion.1 = f32[128,2048]{1,0:T(8,128)} fusion(f32[128,2048]{1,0:T(8,128)S(1)} %fusion.50, bf16[384,2048]{1,0:T(8,128)(2,1)} %bitcast.28, f32[128,384]{1,0:T(8,128)S(1)} %copy-done.3), kind=kOutput, calls=%fused_computation.10 | convolution fusion | flops 201785344 | bytes 3866624 | tf_op jit(solution)/shard_map/dot_general | solution.py:127
  216.8 5.1 %fusion.5 = bf16[128,2048]{1,0:T(8,128)(2,1)} fusion(f32[128,2048]{1,0:T(8,128)} %convolution_add_fusion.1, bf16[704,2048]{1,0:T(8,128)(2,1)S(1)} %copy-done, bf16[128,2048]{1,0:T(8,128)(2,1)S(1)} %reshape.262, bf16[2048,704]{0,1:T(8,128)(2,1)} %param.32, f32[128,704]{0,1:T(8,128)} %fusion.63), kind=kOutput, calls=%fused_computation.12 | convolution fusion | flops 739262464 | bytes 8224768 | tf_op jit(solution)/shard_map/dot_general | solution.py:133
  223.7 18.3 %reduce-scatter.2.cloned.1.call-done = bf16[128,512]{1,0:T(8,128)(2,1)} async-done(((bf16[128,2048]{1,0:T(8,128)(2,1)}), bf16[128,512]{1,0:T(8,128)(2,1)}) %reduce-scatter.2.cloned.1.call-update) | async-done | bytes 131088 | tf_op jit(solution)/shard_map/reduce_scatter | solution.py:134
  241.9 1.6 reshape.268
  (55 shorter events, 11.3 us)
Async XLA Ops:
  7.2 209.6 %copy-start = (bf16[704,2048]{1,0:T(8,128)(2,1)S(1)}, bf16[704,2048]{1,0:T(8,128)(2,1)}, u32[]{:S(2)}) copy-start(bf16[704,2048]{1,0:T(8,128)(2,1)} %param.33) | copy-start | bytes 8650756
  7.2 9.4 %copy-start.7 = (s32[2]{0:T(128)S(1)}, s32[2]{0:T(128)}, u32[]{:S(2)}) copy-start(s32[2]{0:T(128)} %param.22) | copy-start | bytes 28
  7.2 37.8 %all-gather.3.cloned.1.call-start = ((), (), s32[]{:S(2)}) async-start(), calls=%async_computation.3 | async-start | bytes 3538944 | tf_op jit(solution)/shard_map/all_gather | solution.py:46
  9.7 69.5 %all-gather.5.cloned.1.call-start = ((), (), s32[]{:S(2)}) async-start(), calls=%async_computation.4 | async-start | bytes 3538944 | tf_op jit(solution)/shard_map/all_gather | solution.py:58
  12.1 120.3 %all-reduce.2.cloned.1.call-start = ((), (), s32[]{:S(2)}) async-start(), calls=%async_computation.5 | async-start | bytes 1048576 | tf_op jit(solution)/shard_map/psum | solution.py:81
  56.7 1.7 copy-start.1
  87.9 6.3 %copy-start.6 = (f32[64,2,6]{0,1,2:T(2,128)S(1)}, f32[64,2,6]{0,1,2:T(2,128)}, u32[]{:S(2)}) copy-start(f32[64,2,6]{0,1,2:T(2,128)} %param.27) | copy-start | bytes 9220
  93.8 40.9 %copy-start.5 = (f32[2048]{0:T(1024)S(1)}, f32[2048]{0:T(1024)}, u32[]{:S(2)}) copy-start(f32[2048]{0:T(1024)} %param.25) | copy-start | bytes 24580
  133.8 0.8 copy-start.2
  162.4 8.5 %copy-start.4 = (bf16[8,2,24,2048]{3,2,1,0:T(8,128)(2,1)}, bf16[8,2,24,2048]{3,2,1,0:T(8,128)(2,1)S(1)}, u32[]{:S(2)}) copy-start(bf16[8,2,24,2048]{3,2,1,0:T(8,128)(2,1)S(1)} %all_to_all.10) | copy-start | bytes 4718596
  186.6 25.3 %all-to-all-start.1 = ((bf16[8,2,24,2048]{3,2,1,0:T(8,128)(2,1)}), bf16[8,2,24,2048]{3,2,1,0:T(8,128)(2,1)}, u32[]{:S(2)}, u32[]{:S(2)}) async-start(bf16[8,2,24,2048]{3,2,1,0:T(8,128)(2,1)} %copy.83), calls=%async_computation.1 | async-start | bytes 3145728 | tf_op jit(solution)/shard_map/all_to_all | solution.py:124
  190.9 51.0 %reduce-scatter.2.cloned.1.call-start = ((), (), s32[]{:S(2)}) async-start(), calls=%async_computation.6 | async-start | bytes 655360 | tf_op jit(solution)/shard_map/reduce_scatter | solution.py:134
  212.0 2.0 copy-start.3
Sparse Core Ops, SparseCore 0:
  9.9 35.0 all-gather.2
  46.8 32.3 all-gather.4
  93.9 38.3 all-reduce.1
  222.1 19.8 reduce-scatter.1
where the time goes:
time: 251 us; the launch traced here: 250 us
  waiting for transfers between devices  121 us (48%)
  matrix products  44.3 us (18%)
  local copies, waits for them, and re-layouts  31.3 us (12%)
  blocking collectives  24.4 us (10%)
  between operations  14 us (6%)
  other arithmetic  10.7 us (4%)
  starting transfers between devices  4.45 us (2%)
    psum x1, waiting for transfers between devices, body(): lax.psum(attn_part.astype(jnp.bfloat16), 'col').astype(jnp.float32)  37 us
    all_gather x1, waiting for transfers between devices, body(): key_piece = lax.all_gather(keys_here, 'row', axis=0, tiled=True)  28.1 us
    all_to_all x1, blocking collectives, body(): arrived = lax.all_to_all(outgoing, 'row', 0, 0, tiled=True)  24.4 us
    all_gather x1, waiting for transfers between devices, body(): lax.all_gather(values_here, 'row', axis=0, tiled=True)  20 us
    reduce_scatter x1, waiting for transfers between devices, body(): lax.psum_scatter((routed + shared_part).astype(jnp.bfloat16), 'col', scat...  18.3 us
    all_to_all x1, waiting for transfers between devices, body(): lax.all_to_all(expert_out, 'row', 0, 0, tiled=True)  17.5 us
    dot_general x1, matrix products, body(): jnp.einsum('lgnsf,lgfd->nlsd', hidden_act, wd, preferred_element_type=jnp...  12.9 us
    all_gather x1, local copies, waits for them, and re-layouts, body(): key_piece = lax.all_gather(keys_here, 'row', axis=0, tiled=True)  8.71 us
  transfers between devices with their start and end apart: 5, of which 5 were waited for; matrix products, arithmetic and copies ran while one was open for 10% of the time, Pallas kernels for 0%

commit v1 on v0

--- a/solution.py
+++ b/solution.py
@@ -43,7 +43,12 @@
     values_here = jnp.concatenate([cache_values, new_values], axis=0)
     query_heads = queries.reshape(rows_here, requests, heads_here, HD)
     local_pos = row_index * rows_here + jnp.arange(rows_here, dtype=jnp.int32)
-    key_piece = lax.all_gather(keys_here, "row", axis=0, tiled=True)
+    ring = [keys_here]
+    for hop in range(7):
+        ring.append(lax.ppermute(ring[-1], "row", [(dev, (dev + 1) % 8) for dev in range(8)]))
+    key_piece = jnp.roll(
+        jnp.concatenate(ring[::-1], axis=0), (lax.axis_index("row") + 1) * ring[0].shape[0], axis=0
+    )
     key_count = key_piece.shape[0]
     global_row = jnp.arange(key_count, dtype=jnp.int32)
     shard_index = global_row // block_rows

time: 251 us -> 282 us (1.12)
  waiting for transfers between devices: 121 us -> 138 us
  local copies, waits for them, and re-layouts: 31.3 us -> 42.7 us
    ppermute x0 -> x7, waiting for transfers between devices: none -> 65.9 us  [body(): lax.ppermute(ring[-1], 'row', [(dev, (dev + 1) % 8) for dev in range(8)])]
    all_gather x1 -> x0, waiting for transfers between devices: 28.1 us -> none  [body(): key_piece = lax.all_gather(keys_here, 'row', axis=0, tiled=True)]
    all_gather x1, waiting for transfers between devices: 20 us -> 0.01 us  [body(): lax.all_gather(values_here, 'row', axis=0, tiled=True)]
    concatenate x0 -> x1, local copies, waits for them, and re-layouts: none -> 11.8 us  [body(): jnp.roll(jnp.concatenate(ring[::-1], axis=0), (lax.axis_index('row') + 1)...]
    all_gather x1 -> x0, local copies, waits for them, and re-layouts: 8.71 us -> none  [body(): key_piece = lax.all_gather(keys_here, 'row', axis=0, tiled=True)]
    dynamic_slice x0 -> x1, local copies, waits for them, and re-layouts: none -> 3.54 us  [body(): jnp.roll(jnp.concatenate(ring[::-1], axis=0), (lax.axis_index('row') + 1)...]
    unnamed x19 -> x31, local copies, waits for them, and re-layouts: 4.27 us -> 7.43 us
  transfers between devices with their start and end apart: 5 -> 11, of which waited for: 5 -> 10; matrix products, arithmetic and copies ran while one was open for 10% -> 13% of each run, Pallas kernels for 0% -> 0%
where the time goes in v1:
time: 282 us; the launch traced here: 280 us
  waiting for transfers between devices  138 us (49%)
  local copies, waits for them, and re-layouts  42.7 us (15%)
  matrix products  42.3 us (15%)
  blocking collectives  24.4 us (9%)
  between operations  14 us (5%)
  other arithmetic  13.4 us (5%)
  starting transfers between devices  4.92 us (2%)
    ppermute x7, waiting for transfers between devices, body(): lax.ppermute(ring[-1], 'row', [(dev, (dev + 1) % 8) for dev in range(8)])  65.9 us
    psum x1, waiting for transfers between devices, body(): lax.psum(attn_part.astype(jnp.bfloat16), 'col').astype(jnp.float32)  36.1 us
    all_to_all x1, blocking collectives, body(): arrived = lax.all_to_all(outgoing, 'row', 0, 0, tiled=True)  24.4 us
    reduce_scatter x1, waiting for transfers between devices, body(): lax.psum_scatter((routed + shared_part).astype(jnp.bfloat16), 'col', scat...  18.3 us
    all_to_all x1, waiting for transfers between devices, body(): lax.all_to_all(expert_out, 'row', 0, 0, tiled=True)  17.5 us
    dot_general x1, matrix products, body(): jnp.einsum('lgnsf,lgfd->nlsd', hidden_act, wd, preferred_element_type=jnp...  12.9 us
    concatenate x1, local copies, waits for them, and re-layouts, body(): jnp.roll(jnp.concatenate(ring[::-1], axis=0), (lax.axis_index('row') + 1)...  11.8 us
    all_gather x1, local copies, waits for them, and re-layouts, body(): lax.all_gather(values_here, 'row', axis=0, tiled=True)  8.72 us
  transfers between devices with their start and end apart: 11, of which 10 were waited for; matrix products, arithmetic and copies ran while one was open for 13% of the time, Pallas kernels for 0%

profile of v1, /device:TPU:0, one launch (start us, length us, event | category | flops | bytes accessed | tf_op | source)
XLA Modules:
  0.0 279.6 jit_solution(1688120642853457349)
XLA Ops:
  7.2 2.5 pad_maximum_fusion.1
  12.7 9.9 %collective-permute-done = bf16[192,2,512]{0,2,1:T(8,128)(2,1)} collective-permute-done((bf16[192,2,512]{0,2,1:T(8,128)(2,1)S(1)}, bf16[192,2,512]{0,2,1:T(8,128)(2,1)}, u32[]{:S(2)}, u32[]{:S(2)}) %collective-permute-start) | collective-permute-done | bytes 393248 | tf_op jit(solution)/shard_map/ppermute | solution.py:48
  22.8 10.9 %collective-permute-done.1 = bf16[192,2,512]{0,2,1:T(8,128)(2,1)} collective-permute-done((bf16[192,2,512]{0,2,1:T(8,128)(2,1)}, bf16[192,2,512]{0,2,1:T(8,128)(2,1)}, u32[]{:S(2)}, u32[]{:S(2)}) %collective-permute-start.1) | collective-permute-done | bytes 393248 | tf_op jit(solution)/shard_map/ppermute | solution.py:48
  34.3 4.4 %reduce-window.6 = s32[64,6,128]{2,0,1:T(8,128)} reduce-window(s32[64,6,128]{2,0,1:T(8,128)} %fusion.39, s32[]{:T(128)} %constant.91.clone.1), window={size=1x1x128 pad=0_0x0_0x127_0}, to_apply=%region_3.4 | reduce-window | flops 6242304 | bytes 393220 | tf_op jit(solution)/shard_map/reduce-window
  40.0 10.5 %collective-permute-done.2 = bf16[192,2,512]{0,2,1:T(8,128)(2,1)} collective-permute-done((bf16[192,2,512]{0,2,1:T(8,128)(2,1)}, bf16[192,2,512]{0,2,1:T(8,128)(2,1)}, u32[]{:S(2)}, u32[]{:S(2)}) %collective-permute-start.2) | collective-permute-done | bytes 393248 | tf_op jit(solution)/shard_map/ppermute | solution.py:48
  53.4 6.9 %collective-permute-done.3 = bf16[192,2,512]{0,2,1:T(8,128)(2,1)} collective-permute-done((bf16[192,2,512]{0,2,1:T(8,128)(2,1)}, bf16[192,2,512]{0,2,1:T(8,128)(2,1)}, u32[]{:S(2)}, u32[]{:S(2)}) %collective-permute-start.3) | collective-permute-done | bytes 393248 | tf_op jit(solution)/shard_map/ppermute | solution.py:48
  60.4 9.6 %collective-permute-done.4 = bf16[192,2,512]{0,2,1:T(8,128)(2,1)S(1)} collective-permute-done((bf16[192,2,512]{0,2,1:T(8,128)(2,1)}, bf16[192,2,512]{0,2,1:T(8,128)(2,1)S(1)}, u32[]{:S(2)}, u32[]{:S(2)}) %collective-permute-start.4) | collective-permute-done | bytes 393248 | tf_op jit(solution)/shard_map/ppermute | solution.py:48
  70.9 9.4 %collective-permute-done.5 = bf16[192,2,512]{0,2,1:T(8,128)(2,1)S(1)} collective-permute-done((bf16[192,2,512]{0,2,1:T(8,128)(2,1)S(1)}, bf16[192,2,512]{0,2,1:T(8,128)(2,1)S(1)}, u32[]{:S(2)}, u32[]{:S(2)}) %collective-permute-start.5) | collective-permute-done | bytes 393248 | tf_op jit(solution)/shard_map/ppermute | solution.py:48
  81.9 8.8 %collective-permute-done.6 = bf16[192,2,512]{0,2,1:T(8,128)(2,1)} collective-permute-done((bf16[192,2,512]{0,2,1:T(8,128)(2,1)S(1)}, bf16[192,2,512]{0,2,1:T(8,128)(2,1)}, u32[]{:S(2)}, u32[]{:S(2)}) %collective-permute-start.6) | collective-permute-done | bytes 393248 | tf_op jit(solution)/shard_map/ppermute | solution.py:48
  90.8 11.8 %concatenate.14 = bf16[3072,2,512]{0,2,1:T(8,128)(2,1)} concatenate(bf16[192,2,512]{0,2,1:T(8,128)(2,1)} %collective-permute-done.6, bf16[192,2,512]{0,2,1:T(8,128)(2,1)} %copy-done.4, bf16[192,2,512]{0,2,1:T(8,128)(2,1)} %copy-done.3, bf16[192,2,512]{0,2,1:T(8,128)(2,1)} %collective-permute-done.3, bf16[192,2,512]{0,2,1:T(8,128)(2,1)} %collective-permute-done.2, ...), dimensions={0} | concatenate | bytes 12582912 | tf_op jit(solution)/shard_map/jit(_roll_dynamic)/concatenate | solution.py:49
  102.6 3.5 %constant_dynamic-slice_fusion.1 = bf16[1536,2,512]{0,2,1:T(8,128)(2,1)S(1)} fusion(bf16[3072,2,512]{0,2,1:T(8,128)(2,1)} %concatenate.14, s32[]{:T(128)S(6)} %select_n.93), kind=kLoop, calls=%fused_computation.104 | loop fusion | bytes 6291460 | tf_op jit(solution)/shard_map/jit(_roll_dynamic)/dynamic_slice | solution.py:49
  109.7 8.7 %copy.90 = bf16[1536,2,512]{0,2,1:T(8,128)(2,1)} copy(bf16[1536,2,512]{2,1,0:T(2,128)(2,1)} %all-gather.2.cloned.1.call-done) | data formatting | bytes 6291456 | tf_op jit(solution)/shard_map/all_gather | solution.py:63
  118.4 5.9 %fusion.11 = bf16[64,2,2048]{2,0,1:T(8,128)(2,1)} fusion(bf16[4,128,2048,1]{2,1,0,3:T(8,128)(2,1)} %bitcast.123, bf16[1536,2,4,128]{0,3,2,1:T(8,128)(2,1)} %bitcast.116, f32[2,4,64,1536]{3,2,1,0:T(8,128)} %copy-done.1, f32[2,4,64]{2,1,0:T(4,128)S(1)} %broadcast_maximum_fusion, pred[2,64,1536]{2,1,0:T(8,128)(4,1)S(1)} %copy-done.5, f32[2,4,64]{2,1,0:T(4,128)S(1)} %fusion.3), kind=kOutput, calls=%fused_computation.21 | convolution fusion | flops 472514560 | bytes 9113600 | tf_op jit(solution)/shard_map/rhid,hde->ire/dot_general | solution.py:83
  125.8 36.1 %all-reduce.2.cloned.1.call-done = bf16[64,2,2048]{2,0,1:T(8,128)(2,1)} async-done(((bf16[64,2,2048]{2,0,1:T(8,128)(2,1)}), bf16[64,2,2048]{2,0,1:T(8,128)(2,1)}) %all-reduce.2.cloned.1.call-update) | async-done | bytes 524304 | tf_op jit(solution)/shard_map/psum | solution.py:86
  167.6 24.4 %all_to_all.10 = bf16[8,2,24,2048]{3,2,1,0:T(8,128)(2,1)S(1)} all-to-all(bf16[8,2,24,2048]{3,2,1,0:T(8,128)(2,1)S(1)} %bitcast.115), channel_id=1, replica_groups=mesh['row'=8,'col'=4] {'row'}, dimensions={0} | all-to-all | bytes 3145728 | tf_op jit(solution)/shard_map/all_to_all | solution.py:118
  192.0 8.5 %fusion.17 = f32[2,8,24,4,352]{4,2,3,1,0:T(8,128)} fusion(bf16[2,4,2048,352,1]{2,3,1,4,0:T(8,128)(2,1)} %bitcast.120, bf16[8,2,24,2048]{3,2,1,0:T(8,128)(2,1)S(1)} %all_to_all.10), kind=kOutput, calls=%fused_computation.26 | convolution fusion | flops 2214592512 | bytes 15269888 | tf_op jit(solution)/shard_map/nlsd,lgdf->lgnsf/dot_general | solution.py:124
  200.6 12.9 %fusion.2 = bf16[8,2,24,2048]{3,2,0,1:T(8,128)(2,1)} fusion(bf16[2,4,352,2048,1]{3,2,1,4,0:T(8,128)(2,1)} %bitcast.121, f32[2,8,24,4,352]{4,2,3,1,0:T(8,128)} %fusion.17, bf16[2,4,2048,352,1]{2,3,1,4,0:T(8,128)(2,1)} %bitcast.122, bf16[8,2,24,2048]{3,2,1,0:T(8,128)(2,1)} %copy-done.7), kind=kOutput, calls=%fused_computation.6 | convolution fusion | flops 4433215488 | bytes 28377088 | tf_op jit(solution)/shard_map/lgnsf,lgfd->nlsd/dot_general | solution.py:126
  213.5 2.7 copy.102
  216.2 4.3 %all-to-all-start.1 = ((bf16[8,2,24,2048]{3,2,1,0:T(8,128)(2,1)}), bf16[8,2,24,2048]{3,2,1,0:T(8,128)(2,1)}, u32[]{:S(2)}, u32[]{:S(2)}) async-start(bf16[8,2,24,2048]{3,2,1,0:T(8,128)(2,1)} %copy.102), calls=%async_computation.1 | async-start | bytes 3145728 | tf_op jit(solution)/shard_map/all_to_all | solution.py:129
  220.5 3.5 %fusion.63 = f32[128,704]{0,1:T(8,128)} fusion(bf16[128,2048]{1,0:T(8,128)(2,1)S(1)} %reshape.262, bf16[2048,704]{0,1:T(8,128)(2,1)} %param.31), kind=kOutput, calls=%fused_computation.108 | convolution fusion | flops 369098752 | bytes 3768320 | tf_op jit(solution)/shard_map/dot_general | solution.py:135
  224.0 17.5 %all-to-all-done.1 = bf16[8,2,24,2048]{3,2,1,0:T(8,128)(2,1)} async-done(((bf16[8,2,24,2048]{3,2,1,0:T(8,128)(2,1)}), bf16[8,2,24,2048]{3,2,1,0:T(8,128)(2,1)}, u32[]{:S(2)}, u32[]{:S(2)}) %all-to-all-start.1) | async-done | bytes 1572896 | tf_op jit(solution)/shard_map/all_to_all | solution.py:129
  243.5 2.8 %convolution_add_fusion.1 = f32[128,2048]{1,0:T(8,128)} fusion(f32[128,2048]{1,0:T(8,128)S(1)} %fusion.50, bf16[384,2048]{1,0:T(8,128)(2,1)} %bitcast.28, f32[128,384]{1,0:T(8,128)S(1)} %copy-done.6), kind=kOutput, calls=%fused_computation.10 | convolution fusion | flops 201785344 | bytes 3866624 | tf_op jit(solution)/shard_map/dot_general | solution.py:132
  246.3 5.1 %fusion.5 = bf16[128,2048]{1,0:T(8,128)(2,1)} fusion(f32[128,2048]{1,0:T(8,128)} %convolution_add_fusion.1, bf16[704,2048]{1,0:T(8,128)(2,1)S(1)} %copy-done, bf16[128,2048]{1,0:T(8,128)(2,1)S(1)} %reshape.262, bf16[2048,704]{0,1:T(8,128)(2,1)} %param.32, f32[128,704]{0,1:T(8,128)} %fusion.63), kind=kOutput, calls=%fused_computation.12 | convolution fusion | flops 739262464 | bytes 8224768 | tf_op jit(solution)/shard_map/dot_general | solution.py:138
  253.2 18.3 %reduce-scatter.2.cloned.1.call-done = bf16[128,512]{1,0:T(8,128)(2,1)} async-done(((bf16[128,2048]{1,0:T(8,128)(2,1)}), bf16[128,512]{1,0:T(8,128)(2,1)}) %reduce-scatter.2.cloned.1.call-update) | async-done | bytes 131088 | tf_op jit(solution)/shard_map/reduce_scatter | solution.py:139
  (79 shorter events, 26.7 us)
Async XLA Ops:
  7.2 239.2 %copy-start = (bf16[704,2048]{1,0:T(8,128)(2,1)S(1)}, bf16[704,2048]{1,0:T(8,128)(2,1)}, u32[]{:S(2)}) copy-start(bf16[704,2048]{1,0:T(8,128)(2,1)} %param.33) | copy-start | bytes 8650756
  7.2 15.3 %copy-start.10 = (s32[64,2,6]{0,1,2:T(2,128)S(1)}, s32[64,2,6]{0,1,2:T(2,128)}, u32[]{:S(2)}) copy-start(s32[64,2,6]{0,1,2:T(2,128)} %param.26) | copy-start | bytes 9220
  7.2 63.7 %copy-start.12 = (s32[2]{0:T(128)S(1)}, s32[2]{0:T(128)}, u32[]{:S(2)}) copy-start(s32[2]{0:T(128)} %param.22) | copy-start | bytes 28
  7.2 102.5 %all-gather.2.cloned.1.call-start = ((), (), s32[]{:S(2)}) async-start(), calls=%async_computation.3 | async-start | bytes 3538944 | tf_op jit(solution)/shard_map/all_gather | solution.py:63
  9.7 152.2 %all-reduce.2.cloned.1.call-start = ((), (), s32[]{:S(2)}) async-start(), calls=%async_computation.4 | async-start | bytes 1048576 | tf_op jit(solution)/shard_map/psum | solution.py:86
  12.2 10.4 %collective-permute-start = (bf16[192,2,512]{0,2,1:T(8,128)(2,1)S(1)}, bf16[192,2,512]{0,2,1:T(8,128)(2,1)}, u32[]{:S(2)}, u32[]{:S(2)}) collective-permute-start(bf16[192,2,512]{0,2,1:T(8,128)(2,1)S(1)} %pad_maximum_fusion), channel_id=1, source_target_pairs={{0,4},{4,8},{8,12},{12,16},{16,20},{20,24},{24,28},{28,0},{1,5},{5... | collective-permute-start | bytes 1179656 | tf_op jit(solution)/shard_map/ppermute | solution.py:48
  22.5 11.1 %collective-permute-start.1 = (bf16[192,2,512]{0,2,1:T(8,128)(2,1)}, bf16[192,2,512]{0,2,1:T(8,128)(2,1)}, u32[]{:S(2)}, u32[]{:S(2)}) collective-permute-start(bf16[192,2,512]{0,2,1:T(8,128)(2,1)} %collective-permute-done), channel_id=1, source_target_pairs={{0,4},{4,8},{8,12},{12,16},{16,20},{20,24},{24,28},{28,0},{1,5},{5... | collective-permute-start | bytes 1179656 | tf_op jit(solution)/shard_map/ppermute | solution.py:48
  33.6 16.8 %collective-permute-start.2 = (bf16[192,2,512]{0,2,1:T(8,128)(2,1)}, bf16[192,2,512]{0,2,1:T(8,128)(2,1)}, u32[]{:S(2)}, u32[]{:S(2)}) collective-permute-start(bf16[192,2,512]{0,2,1:T(8,128)(2,1)} %collective-permute-done.1), channel_id=1, source_target_pairs={{0,4},{4,8},{8,12},{12,16},{16,20},{20,24},{24,28},{28,0},{1,5},{5... | collective-permute-start | bytes 1179656 | tf_op jit(solution)/shard_map/ppermute | solution.py:48
  50.5 9.8 %collective-permute-start.3 = (bf16[192,2,512]{0,2,1:T(8,128)(2,1)}, bf16[192,2,512]{0,2,1:T(8,128)(2,1)}, u32[]{:S(2)}, u32[]{:S(2)}) collective-permute-start(bf16[192,2,512]{0,2,1:T(8,128)(2,1)} %collective-permute-done.2), channel_id=1, source_target_pairs={{0,4},{4,8},{8,12},{12,16},{16,20},{20,24},{24,28},{28,0},{1,5},{5... | collective-permute-start | bytes 1179656 | tf_op jit(solution)/shard_map/ppermute | solution.py:48
  60.3 9.7 %collective-permute-start.4 = (bf16[192,2,512]{0,2,1:T(8,128)(2,1)}, bf16[192,2,512]{0,2,1:T(8,128)(2,1)S(1)}, u32[]{:S(2)}, u32[]{:S(2)}) collective-permute-start(bf16[192,2,512]{0,2,1:T(8,128)(2,1)} %collective-permute-done.3), channel_id=1, source_target_pairs={{0,4},{4,8},{8,12},{12,16},{16,20},{20,24},{24,28},{28,0},{1,5},{5... | collective-permute-start | bytes 1179656 | tf_op jit(solution)/shard_map/ppermute | solution.py:48
  70.0 0.8 copy-start.3
  70.8 9.5 %collective-permute-start.5 = (bf16[192,2,512]{0,2,1:T(8,128)(2,1)S(1)}, bf16[192,2,512]{0,2,1:T(8,128)(2,1)S(1)}, u32[]{:S(2)}, u32[]{:S(2)}) collective-permute-start(bf16[192,2,512]{0,2,1:T(8,128)(2,1)S(1)} %collective-permute-done.4), channel_id=1, source_target_pairs={{0,4},{4,8},{8,12},{12,16},{16,20},{20,24},{24,28},{28,0},{1,5},{5... | collective-permute-start | bytes 1179656 | tf_op jit(solution)/shard_map/ppermute | solution.py:48
  80.3 0.8 copy-start.4
  81.2 9.6 %collective-permute-start.6 = (bf16[192,2,512]{0,2,1:T(8,128)(2,1)S(1)}, bf16[192,2,512]{0,2,1:T(8,128)(2,1)}, u32[]{:S(2)}, u32[]{:S(2)}) collective-permute-start(bf16[192,2,512]{0,2,1:T(8,128)(2,1)S(1)} %collective-permute-done.5), channel_id=1, source_target_pairs={{0,4},{4,8},{8,12},{12,16},{16,20},{20,24},{24,28},{28,0},{1,5},{5... | collective-permute-start | bytes 1179656 | tf_op jit(solution)/shard_map/ppermute | solution.py:48
  102.6 3.6 %copy-start.5 = (pred[2,64,1536]{2,1,0:T(8,128)(4,1)S(1)}, pred[2,64,1536]{2,1,0:T(8,128)(4,1)}, u32[]{:S(2)}) copy-start(pred[2,64,1536]{2,1,0:T(8,128)(4,1)} %broadcast_or_fusion) | copy-start | bytes 589828
  102.6 3.6 %copy-start.8 = (bf16[64,2,4,128]{3,2,1,0:T(4,128)(2,1)S(1)}, bf16[64,2,4,128]{3,2,1,0:T(4,128)(2,1)}, u32[]{:S(2)}) copy-start(bf16[64,2,4,128]{3,2,1,0:T(4,128)(2,1)} %reshape.257) | copy-start | bytes 393220
  107.2 1.7 copy-start.1
  118.4 6.3 %copy-start.11 = (f32[64,2,6]{0,1,2:T(2,128)S(1)}, f32[64,2,6]{0,1,2:T(2,128)}, u32[]{:S(2)}) copy-start(f32[64,2,6]{0,1,2:T(2,128)} %param.27) | copy-start | bytes 9220
  124.3 40.0 %copy-start.9 = (f32[2048]{0:T(1024)S(1)}, f32[2048]{0:T(1024)}, u32[]{:S(2)}) copy-start(f32[2048]{0:T(1024)} %param.25) | copy-start | bytes 24580
  163.4 0.8 copy-start.2
  192.0 8.5 %copy-start.7 = (bf16[8,2,24,2048]{3,2,1,0:T(8,128)(2,1)}, bf16[8,2,24,2048]{3,2,1,0:T(8,128)(2,1)S(1)}, u32[]{:S(2)}) copy-start(bf16[8,2,24,2048]{3,2,1,0:T(8,128)(2,1)S(1)} %all_to_all.10) | copy-start | bytes 4718596
  216.2 25.3 %all-to-all-start.1 = ((bf16[8,2,24,2048]{3,2,1,0:T(8,128)(2,1)}), bf16[8,2,24,2048]{3,2,1,0:T(8,128)(2,1)}, u32[]{:S(2)}, u32[]{:S(2)}) async-start(bf16[8,2,24,2048]{3,2,1,0:T(8,128)(2,1)} %copy.102), calls=%async_computation.1 | async-start | bytes 3145728 | tf_op jit(solution)/shard_map/all_to_all | solution.py:129
  220.5 51.0 %reduce-scatter.2.cloned.1.call-start = ((), (), s32[]{:S(2)}) async-start(), calls=%async_computation.5 | async-start | bytes 655360 | tf_op jit(solution)/shard_map/reduce_scatter | solution.py:139
  241.5 2.0 copy-start.6
Sparse Core Ops, SparseCore 0:
  9.9 38.6 all-gather.1
  124.4 37.4 all-reduce.1
  251.6 19.8 reduce-scatter.1
